TPU v7x, 32 devices: a whole 2x2x4 slice. The times are simulated.
32 devices in a mesh: mix: 2 (over x), seq: 16 (over z, y, core).
Axes of the slice: x: 2, y: 2, z: 4, core: 2. Of those that a mesh axis runs over, the one named last changes fastest.
Arguments:
- frames: bfloat16 [4096, 1024], P(('mix', 'seq')), parts along dimension 0, may hold values from -18 to 18
- segment_ids: int32 [4096], P(('mix', 'seq')), parts along dimension 0, may hold values from 0 to 2, never falling along the last dimension, each value on 1 to 1500 neighbouring positions
- out_grad: bfloat16 [4096, 1024], P(('mix', 'seq')), parts along dimension 0, may hold values from -6 to 6
- ln_gain: float32 [2048], P(('mix', 'seq')), parts along dimension 0, may hold values from 0.5 to 2
- w_in: bfloat16 [2048, 2048], P(('mix', 'seq')), parts along dimension 0, may hold values from -0.1875 to 0.1875
- dw_kernel: float32 [62, 1024], P('mix', 'seq'), parts along dimension 0, may hold values from -1 to 1
- bn_gain: float32 [2048], P(('mix', 'seq')), parts along dimension 0, may hold values from 0.5 to 2
- bn_bias: float32 [2048], P(('mix', 'seq')), parts along dimension 0, may hold values from -3 to 3
- w_out: bfloat16 [2048, 1024], P(('mix', 'seq')), parts along dimension 0, may hold values from -0.1875 to 0.1875
Outputs:
- outputs: bfloat16 [4096, 1024], P(('mix', 'seq')), parts along dimension 0
- grad_frames: bfloat16 [4096, 1024], P(('mix', 'seq')), parts along dimension 0
- grad_w_in: float32 [2048, 2048], P(('mix', 'seq')), parts along dimension 0
- grad_w_out: float32 [2048, 1024], P(('mix', 'seq')), parts along dimension 0
- grad_kernel: float32 [62, 1024], P('mix', 'seq'), parts along dimension 0
- grad_ln_gain: float32 [2048], P(('mix', 'seq')), parts along dimension 0
- grad_bn_gain: float32 [2048], P(('mix', 'seq')), parts along dimension 0
- grad_bn_bias: float32 [2048], P(('mix', 'seq')), parts along dimension 0
There are 2 independent parts, one for each index of `mix`. A program takes and returns all parts, laid end to end along the dimension named above; each array names one. Nothing has to cross between parts.
Inputs may be any that keep to these rules, and one draw needn't show every extreme that they name: `segment_ids`: ids never fall along the stream; every utterance number is used, by 1 to 1500 consecutive frames, one utterance exactly 1500.
All inputs are finite; a program needn't handle non-finite values.
Results may differ from a plain program's by a relative error of at most 0.012.
The roundings to bfloat16 on the way count: a program that leaves them out, or rounds other values in their place, can miss the bound.
Values may be sent and summed in bfloat16 or wider, within the bound.
No kernel may reach another device: no remote copies, remote signals or barrier semaphores. Data moves between devices by JAX's collectives and lax.ppermute only.
A program may use at most 128 MiB of HBM per device.

v0:
```python
import math
import jax
import jax.numpy as jnp
from jax import lax
from jax.sharding import PartitionSpec as P

EPSILON = 1e-05


def with_halo(cells, sides, width):
    for axis, dim in sides:
        count = lax.axis_size(axis)
        ends = count - 1
        head = lax.slice_in_dim(cells, 0, width, axis=dim)
        tail = lax.slice_in_dim(cells, cells.shape[dim] - width, cells.shape[dim], axis=dim)
        cells = jnp.concatenate(
            [
                lax.ppermute(tail, axis, [(i, (i + 1) % count) for i in range(ends)]),
                cells,
                lax.ppermute(head, axis, [((i + 1) % count, i) for i in range(ends)]),
            ],
            axis=dim,
        )
    return cells


def local(frames, segment_ids, out_grad, ln_gain, w_in, dw_kernel, bn_gain, bn_bias, w_out):
    frame_count = frames.shape[0]
    width = frames.shape[1]
    taps = dw_kernel.shape[0]
    margin = taps // 2
    devices = lax.axis_size("seq")
    stream = frame_count * devices
    grad_scale = 1.0 / math.sqrt(stream)
    share = width // devices
    gains, kernel, bn_scale, bn_shift = (
        lax.all_gather(ln_gain, "seq", axis=0, tiled=True),
        lax.all_gather(dw_kernel, "seq", axis=1, tiled=True),
        lax.all_gather(bn_gain, "seq", axis=0, tiled=True),
        lax.all_gather(bn_bias, "seq", axis=0, tiled=True),
    )
    own_ids = segment_ids + 1
    padded_ids = with_halo(own_ids, (("seq", 0),), margin)
    masks = [
        (padded_ids[tap_index : tap_index + frame_count] == own_ids).astype(jnp.float32)[:, None]
        for tap_index in range(taps)
    ]
    frames_float = frames.astype(jnp.float32)
    mean_ln = jnp.mean(frames_float, axis=1, keepdims=True)
    centred = frames_float - mean_ln
    rstd_ln = lax.rsqrt(jnp.mean(centred * centred, axis=1, keepdims=True) + EPSILON)
    ln_hat = centred * rstd_ln
    ln_x = (ln_hat * gains).astype(jnp.bfloat16)
    columns = ln_x
    hidden = jnp.dot(
        columns, lax.all_gather(w_in, "seq", axis=0, tiled=True), preferred_element_type=jnp.float32
    )
    left_half = hidden[:, :width]
    right_gate = jax.nn.sigmoid(hidden[:, width:])
    glu = (left_half * right_gate).astype(jnp.bfloat16)
    padded_glu = with_halo(glu, (("seq", 0),), margin)
    conv_out = jnp.zeros((frame_count, width), jnp.float32)
    for tap_index in range(taps):
        conv_out = (
            conv_out
            + kernel[tap_index]
            * padded_glu[tap_index : tap_index + frame_count].astype(jnp.float32)
            * masks[tap_index]
        )
    plain_sums, square_sums = lax.psum(
        (jnp.sum(conv_out, axis=0), jnp.sum(conv_out * conv_out, axis=0)), "seq"
    )
    bn_mean = plain_sums / stream
    bn_var = square_sums / stream - bn_mean * bn_mean
    bn_rstd = lax.rsqrt(bn_var + EPSILON)
    bn_hat = (conv_out - bn_mean) * bn_rstd
    zed = bn_hat * bn_scale + bn_shift
    zed_gate = jax.nn.sigmoid(zed)
    activation = (zed * zed_gate).astype(jnp.bfloat16)
    columns = activation
    projected = jnp.dot(
        columns,
        lax.all_gather(w_out, "seq", axis=0, tiled=True),
        preferred_element_type=jnp.float32,
    )
    outputs = (frames_float + projected).astype(jnp.bfloat16)
    grad_w_out = lax.psum_scatter(
        jnp.einsum("fa,fb->ab", activation, out_grad, preferred_element_type=jnp.float32)
        * grad_scale,
        "seq",
        scatter_dimension=0,
        tiled=True,
    )
    grad_act = jnp.einsum(
        "fe,ne->fn",
        out_grad,
        lax.all_gather(w_out, "seq", axis=0, tiled=True),
        preferred_element_type=jnp.float32,
    )
    grad_zed = grad_act * zed_gate * (1.0 + zed * (1.0 - zed_gate))
    bias_total, gain_total = lax.psum(
        (jnp.sum(grad_zed, axis=0), jnp.sum(grad_zed * bn_hat, axis=0)), "seq"
    )
    grad_conv = bn_scale * bn_rstd * (grad_zed - bias_total / stream - bn_hat * gain_total / stream)
    first_channel = lax.axis_index("seq") * share
    grad_bn_bias = lax.dynamic_slice_in_dim(bias_total, first_channel, share, 0) * grad_scale
    grad_bn_gain = lax.dynamic_slice_in_dim(gain_total, first_channel, share, 0) * grad_scale
    kernel_rows = [
        jnp.sum(
            grad_conv
            * padded_glu[tap_index : tap_index + frame_count].astype(jnp.float32)
            * masks[tap_index],
            axis=0,
        )
        for tap_index in range(taps)
    ]
    kernel_term = jnp.stack(kernel_rows) * grad_scale
    padded_conv = with_halo(grad_conv, (("seq", 0),), margin)
    grad_glu = jnp.zeros((frame_count, width), jnp.float32)
    for tap_index in range(taps):
        mirror = 2 * margin - tap_index
        grad_glu = (
            grad_glu
            + kernel[tap_index] * padded_conv[mirror : mirror + frame_count] * masks[mirror]
        )
    grad_hidden = jnp.concatenate(
        [grad_glu * right_gate, grad_glu * left_half * right_gate * (1.0 - right_gate)], axis=1
    ).astype(jnp.bfloat16)
    grad_ln = jnp.einsum(
        "fe,ne->fn",
        grad_hidden,
        lax.all_gather(w_in, "seq", axis=0, tiled=True),
        preferred_element_type=jnp.float32,
    )
    in_term = (
        jnp.einsum("fa,fb->ab", ln_x, grad_hidden, preferred_element_type=jnp.float32) * grad_scale
    )
    gain_term = jnp.sum(grad_ln * ln_hat, axis=0) * grad_scale
    grad_w_in, grad_kernel, grad_ln_gain = (
        lax.psum_scatter(in_term, "seq", scatter_dimension=0, tiled=True),
        lax.psum_scatter(kernel_term, "seq", scatter_dimension=1, tiled=True),
        lax.psum_scatter(gain_term, "seq", scatter_dimension=0, tiled=True),
    )
    grad_hat = grad_ln * gains
    grad_input = rstd_ln * (
        grad_hat
        - jnp.mean(grad_hat, axis=1, keepdims=True)
        - ln_hat * jnp.mean(grad_hat * ln_hat, axis=1, keepdims=True)
    )
    grad_frames = (out_grad.astype(jnp.float32) + grad_input).astype(jnp.bfloat16)
    return (
        outputs,
        grad_frames,
        grad_w_in,
        grad_w_out,
        grad_kernel,
        grad_ln_gain,
        grad_bn_gain,
        grad_bn_bias,
    )


def solution(mesh):
    return jax.shard_map(
        local,
        mesh=mesh,
        in_specs=(
            P(("mix", "seq"), None),
            P(("mix", "seq")),
            P(("mix", "seq"), None),
            P(("mix", "seq")),
            P(("mix", "seq"), None),
            P("mix", "seq"),
            P(("mix", "seq")),
            P(("mix", "seq")),
            P(("mix", "seq"), None),
        ),
        out_specs=(
            P(("mix", "seq"), None),
            P(("mix", "seq"), None),
            P(("mix", "seq"), None),
            P(("mix", "seq"), None),
            P("mix", "seq"),
            P(("mix", "seq")),
            P(("mix", "seq")),
            P(("mix", "seq")),
        ),
        check_vma=False,
    )
```

profile of v0, /device:TPU:0, one launch (start us, length us, event | category | flops | bytes accessed | tf_op | source)
XLA Modules:
  0.0 432.6 jit_solution(1981038902537433708)
XLA Ops:
  7.2 0.7 all-gather.4.cloned.1.call-update
  7.9 0.7 all-gather.6.cloned.1.call-update
  8.7 0.7 broadcast_add_fusion
  9.4 2.3 collective-permute-start.1
  11.8 1.3 collective-permute-start.3
  13.1 26.5 %all-gather = f32[16,64,31]{1,2,0:T(8,128)S(1)} all-gather(f32[1,64,31]{1,2,0:T(8,128)} %bitcast.175), channel_id=1, replica_groups=mesh['mix'=2,'seq'=16] {'seq'}, dimensions={0}, use_global_device_ids=true | all-gather | bytes 134912 | tf_op jit(solution)/shard_map/all_gather | solution.py:38
  39.6 0.2 copy.18
  39.9 1.3 fusion.301
  41.9 0.9 dynamic-update-slice.2
  42.7 0.8 dynamic-update-slice
  43.6 30.2 %all-reduce = f32[1024]{0:T(1024)S(1)} all-reduce(f32[1024]{0:T(1024)S(1)} %dynamic-update-slice), channel_id=1, replica_groups=mesh['mix'=2,'seq'=16] {'seq'}, use_global_device_ids=true, to_apply=%add | all-reduce | flops 1024 | bytes 8192
  73.8 1.1 convert_reduce_fusion
  74.9 1.2 fusion.129
  76.2 0.9 dynamic-update-slice.1
  77.1 0.7 compare_convert_fusion.29
  77.9 3.1 fusion.291
  81.2 1.5 collective-permute-start
  82.7 1.3 collective-permute-start.2
  84.1 1.7 collective-permute-done.2
  85.8 4.7 %fusion.294 = (f32[1024]{0:T(1024)S(1)}, f32[1024]{0:T(1024)S(1)}, f32[128,1024]{1,0:T(8,128)S(1)}) fusion(f32[128]{0:T(128)S(1)} %get-tuple-element.110, bf16[15,1024]{1,0:T(8,128)(2,1)S(1)} %collective-permute-done.2, bf16[128,1024]{1,0:T(8,128)(2,1)S(1)} %multiply_convert_fusion.3, f32[1024]{0:T(1024)S(1)} %bitcast.107, f32[128]{0:T(128)S(1)} %get-tuple-element.111, ...), kind=kLoop, calls=%fused_computation.505 | loop fusion | flops 28178432 | bytes 998400 | tf_op jit(solution)/shard_map/reduce_sum | solution.py:71
  90.5 59.8 %all-reduce.5 = (f32[1024]{0:T(1024)S(1)}, f32[1024]{0:T(1024)S(1)}, f32[1024]{0:T(1024)S(1)}, f32[1024]{0:T(1024)S(1)}) all-reduce(f32[1024]{0:T(1024)S(1)} %dynamic-update-slice.2, f32[1024]{0:T(1024)S(1)} %dynamic-update-slice.1, f32[1024]{0:T(1024)S(1)} %get-tuple-element.45, ...), channel_id=1, replica_groups=mesh['mix'=2,'seq'=16] {'seq'}, use_global_device_ids=true, to_apply=%add.2 | all-reduce | flops 4096 | bytes 32768
  150.3 2.5 fusion.293
  152.8 30.0 %all-reduce.4 = (f32[1024]{0:T(1024)S(1)}, f32[1024]{0:T(1024)S(1)}) all-reduce(f32[1024]{0:T(1024)S(1)} %get-tuple-element.43, f32[1024]{0:T(1024)S(1)} %get-tuple-element.42), channel_id=1, replica_groups=mesh['mix'=2,'seq'=16] {'seq'}, use_global_device_ids=true, to_apply=%region_9.0 | all-reduce | flops 2048 | bytes 16384 | tf_op jit(solution)/shard_map/psum | solution.py:101
  182.8 0.9 fusion.250
  183.7 0.3 fusion.162
  184.0 0.4 fusion.208
  184.4 0.7 fusion.247
  185.1 0.7 fusion.180
  185.8 0.7 fusion.198
  186.5 0.2 stack.127
  186.7 1.0 copy.19
  187.8 2.7 convolution_multiply_fusion.1
  190.6 0.2 reduce-scatter.6.cloned.1.call-start
  190.8 1.3 collective-permute-start.4
  192.1 3.0 collective-permute-start.5
  195.2 0.9 collective-permute-done.5
  196.1 4.3 %multiply_convert_fusion.1 = (bf16[128,1024]{1,0:T(8,128)(2,1)S(1)}, f32[128,1024]{1,0:T(8,128)S(1)}) fusion(f32[128,2048]{1,0:T(8,128)S(1)} %fusion.291, f32[128]{0:T(128)S(1)} %get-tuple-element.94, f32[128,1024]{1,0:T(8,128)S(1)} %get-tuple-element.52, f32[15,1024]{1,0:T(8,128)S(1)} %collective-permute-done.5, f32[1024]{0:T(1024)S(1)} %bitcast.108, ...), kind=kLoop, calls=%fused_computation.415 | loop fusion | flops 16515072 | bytes 2100224 | tf_op jit(solution)/shard_map/convert
  200.4 0.2 multiply_convert_fusion
  200.6 4.6 %convolution_multiply_fusion = f32[1024,2048]{1,0:T(8,128)} fusion(bf16[128,1024]{1,0:T(8,128)(2,1)S(1)} %multiply_convert_fusion, bf16[128,1024]{1,0:T(8,128)(2,1)S(1)} %get-tuple-element.53, bf16[128,1024]{1,0:T(8,128)(2,1)S(1)} %copy-done, f32[1024]{0:T(1024)S(1)} %all-reduce, f32[128]{0:T(128)S(1)} %add_rsqrt_fusion.1, f32[128]{0:T(128)S(1)} %broadcast_multiply_fusion.6), kind=kOutput, calls=%fused_computation | convolution fusion | flops 540672000 | bytes 9180160 | tf_op jit(solution)/shard_map/fa,fb->ab/dot_general | solution.py:136
  205.9 0.6 dynamic-slice_multiply_fusion
  206.5 3.1 fusion.1
  209.6 1.6 fusion.128
  211.3 31.1 %all-reduce.3 = f32[1024]{0:T(1024)S(1)} all-reduce(f32[1024]{0:T(1024)S(1)} %broadcast_multiply_fusion.1), channel_id=5, replica_groups=mesh['mix'=2,'seq'=16] {'seq'}, use_global_device_ids=true, to_apply=%region_47.0.clone | all-reduce | flops 1024 | bytes 8192
  242.4 0.6 dynamic-slice.4
  243.0 1.0 fusion.127
  244.0 1.4 copy.20
  245.4 72.5 %reduce-scatter.8.cloned.1.call-done = f32[64,1024]{1,0:T(8,128)} async-done(((f32[1024,1024]{1,0:T(8,128)}), f32[64,1024]{1,0:T(8,128)}) %reduce-scatter.8.cloned.1.call-update) | async-done | bytes 262160 | tf_op jit(solution)/shard_map/reduce_scatter | solution.py:87
  317.9 108.2 %reduce-scatter.6.cloned.1.call-done = f32[64,2048]{1,0:T(8,128)} async-done(((f32[1024,2048]{1,0:T(8,128)}), f32[64,2048]{1,0:T(8,128)}) %reduce-scatter.6.cloned.1.call-update) | async-done | bytes 524304 | tf_op jit(solution)/shard_map/reduce_scatter | solution.py:140
  (41 shorter events, 0.9 us)
Async XLA Ops:
  7.2 70.7 %all-gather.4.cloned.1.call-start = ((), (), s32[]{:S(2)}) async-start(), calls=%async_computation.3 | async-start | bytes 4456448 | tf_op jit(solution)/shard_map/all_gather | solution.py:56
  7.9 142.4 %all-gather.6.cloned.1.call-start = ((), (), s32[]{:S(2)}) async-start(), calls=%async_computation.4 | async-start | bytes 2228224 | tf_op jit(solution)/shard_map/all_gather | solution.py:83
  8.6 235.3 %reduce-scatter.10.cloned.1.call-start = ((), (), s32[]{:S(2)}) async-start(), calls=%async_computation.7 | async-start | bytes 557056
  9.4 67.6 %collective-permute-start.1 = (s32[15]{0:T(128)S(1)}, s32[15]{0:T(128)S(1)}, u32[]{:S(2)}, u32[]{:S(2)}) collective-permute-start(s32[15]{0:T(128)S(1)} %get-tuple-element.128), channel_id=1, source_target_pairs={{0,1},{1,2},{2,3},{3,4},{4,5},{5,6},{6,7},{7,8},{8,9},{9,10},{10,1... | collective-permute-start | bytes 188 | tf_op jit(solution)/shard_map/ppermute | solution.py:18
  11.8 65.3 %collective-permute-start.3 = (s32[15]{0:T(128)S(1)}, s32[15]{0:T(128)S(1)}, u32[]{:S(2)}, u32[]{:S(2)}) collective-permute-start(s32[15]{0:T(128)S(1)} %get-tuple-element.129), channel_id=1, source_target_pairs={{1,0},{2,1},{3,2},{4,3},{5,4},{6,5},{7,6},{8,7},{9,8},{10,9},{11,1... | collective-permute-start | bytes 188 | tf_op jit(solution)/shard_map/ppermute | solution.py:20
  39.7 44.3 %copy-start.3 = (s32[128]{0:T(128)S(1)}, s32[128]{0:T(128)}, u32[]{:S(2)}) copy-start(s32[128]{0:T(128)} %param.10) | copy-start | bytes 1540
  76.1 74.2 %copy-start.2 = (bf16[128,1024]{1,0:T(8,128)(2,1)S(1)}, bf16[128,1024]{1,0:T(8,128)(2,1)}, u32[]{:S(2)}) copy-start(bf16[128,1024]{1,0:T(8,128)(2,1)} %param.11) | copy-start | bytes 786436
  81.2 2.9 collective-permute-start
  82.7 3.1 collective-permute-start.2
  187.8 130.1 %reduce-scatter.8.cloned.1.call-start = ((), (), s32[]{:S(2)}) async-start(), calls=%async_computation.6 | async-start | bytes 4456448 | tf_op jit(solution)/shard_map/reduce_scatter | solution.py:87
  190.6 10.0 %copy-start = (bf16[128,1024]{1,0:T(8,128)(2,1)S(1)}, bf16[128,1024]{1,0:T(8,128)(2,1)}, u32[]{:S(2)}) copy-start(bf16[128,1024]{1,0:T(8,128)(2,1)} %param.9) | copy-start | bytes 786436
  190.6 235.5 %reduce-scatter.6.cloned.1.call-start = ((), (), s32[]{:S(2)}) async-start(), calls=%async_computation.5 | async-start | bytes 8912896 | tf_op jit(solution)/shard_map/reduce_scatter | solution.py:140
  190.8 4.3 %collective-permute-start.4 = (f32[15,1024]{1,0:T(8,128)S(1)}, f32[15,1024]{1,0:T(8,128)S(1)}, u32[]{:S(2)}, u32[]{:S(2)}) collective-permute-start(f32[15,1024]{1,0:T(8,128)S(1)} %get-tuple-element.56), channel_id=1, source_target_pairs={{1,0},{2,1},{3,2},{4,3},{5,4},{6,5},{7,6},{8,7},{9,8},{10,9},{11,1... | collective-permute-start | bytes 184328 | tf_op jit(solution)/shard_map/ppermute | solution.py:20
  192.1 3.9 collective-permute-start.5
  205.9 3.7 copy-start.1
Sparse Core Ops, SparseCore 0:
  10.2 54.4 all-gather.3
  66.8 39.9 all-gather.5
  187.9 53.3 reduce-scatter.9
  246.1 71.7 reduce-scatter.7
  322.4 103.6 reduce-scatter.5
where the time goes:
time: 433 us
  waiting for transfers between devices  185 us (43%)
  blocking collectives  178 us (41%)
  other arithmetic  18.4 us (4%)
  matrix products  17.7 us (4%)
  between operations  15.4 us (4%)
  starting transfers between devices  11.1 us (3%)
  local copies, waits for them, and re-layouts  7.65 us (2%)
    unnamed x3, blocking collectives  121 us
    reduce_scatter x1, waiting for transfers between devices, local(): lax.psum_scatter(in_term, 'seq', scatter_dimension=0, tiled=True)  108 us
    reduce_scatter x1, waiting for transfers between devices, local(): lax.psum_scatter(jnp.einsum('fa,fb->ab', activation, out_grad, preferred_...  72.5 us
    psum x1, blocking collectives, local(): lax.psum((jnp.sum(grad_zed, axis=0), jnp.sum(grad_zed * bn_hat, axis=0)),...  30 us
    all_gather x1, blocking collectives, local(): lax.all_gather(dw_kernel, 'seq', axis=1, tiled=True)  26.5 us
  transfers between devices with their start and end apart: 11, of which 4 were waited for; matrix products, arithmetic and copies ran while one was open for 8% of the time, Pallas kernels for 0%

commit v1 on v0

--- a/solution.py
+++ b/solution.py
@@ -5,6 +5,32 @@
 from jax.sharding import PartitionSpec as P
 
 EPSILON = 1e-05
+
+
+def play_surface(row_data, which_dim):
+    step_out = list(row_data.shape[1:])
+    step_out[which_dim] *= row_data.shape[0]
+    return jnp.moveaxis(row_data, 0, which_dim).reshape(step_out)
+
+
+def bench_launch(values, named_axis, dim_at):
+    parts_n = jax.lax.psum(1, named_axis)
+    xs_all = [(j, (j + 1) % parts_n) for j in range(parts_n)]
+    vals = [(dev_j, d) for d, dev_j in xs_all]
+    low, after = ([], [])
+    for nth in range(parts_n - 1):
+        if nth % 2 == 0:
+            m_next = jax.lax.ppermute(low[-1] if low else values, named_axis, perm=xs_all)
+            low.append(m_next)
+        else:
+            view_out = jax.lax.ppermute(after[-1] if after else values, named_axis, vals)
+            after.append(view_out)
+    z1 = jnp.stack([*low[::-1], values, *after])
+    all_values = jax.lax.axis_index(named_axis)
+    local_next = len(low)
+    mid_arr = all_values - local_next
+    z1 = z1[(jnp.arange(parts_n) - mid_arr) % parts_n]
+    return play_surface(z1, dim_at)
 
 
 def with_halo(cells, sides, width):
@@ -35,7 +61,7 @@
     share = width // devices
     gains, kernel, bn_scale, bn_shift = (
         lax.all_gather(ln_gain, "seq", axis=0, tiled=True),
-        lax.all_gather(dw_kernel, "seq", axis=1, tiled=True),
+        bench_launch(dw_kernel, "seq", 1),
         lax.all_gather(bn_gain, "seq", axis=0, tiled=True),
         lax.all_gather(bn_bias, "seq", axis=0, tiled=True),
     )

time: 433 us -> 455 us (1.051)
  starting transfers between devices: 11.1 us -> 39.3 us
  blocking collectives: 178 us -> 159 us
  waiting for transfers between devices: 185 us -> 192 us
    ppermute x0 -> x15, starting transfers between devices: none -> 29.7 us  [the longest x7 27.5 us: bench_launch(): jax.lax.ppermute(after[-1] if after else values, named_axis, vals)]
    all_gather x1 -> x0, blocking collectives: 26.5 us -> none  [local(): lax.all_gather(dw_kernel, 'seq', axis=1, tiled=True)]
    ppermute x0 -> x15, waiting for transfers between devices: none -> 9.73 us  [the longest x8 7.05 us: bench_launch(): jax.lax.ppermute(low[-1] if low else values, named_axis, perm=xs_all)]
    unnamed x3, blocking collectives: 121 us -> 129 us
  transfers between devices with their start and end apart: 11 -> 26, of which waited for: 4 -> 12; matrix products, arithmetic and copies ran while one was open for 8% -> 9% of each run, Pallas kernels for 0% -> 0%
where the time goes in v1:
time: 455 us
  waiting for transfers between devices  192 us (42%)
  blocking collectives  159 us (35%)
  starting transfers between devices  39.3 us (9%)
  other arithmetic  19.2 us (4%)
  matrix products  17.8 us (4%)
  between operations  15.5 us (3%)
  local copies, waits for them, and re-layouts  11.5 us (3%)
    unnamed x3, blocking collectives  129 us
    reduce_scatter x1, waiting for transfers between devices, local(): lax.psum_scatter(in_term, 'seq', scatter_dimension=0, tiled=True)  108 us
    reduce_scatter x1, waiting for transfers between devices, local(): lax.psum_scatter(jnp.einsum('fa,fb->ab', activation, out_grad, preferred_...  72.4 us
    psum x1, blocking collectives, local(): lax.psum((jnp.sum(grad_zed, axis=0), jnp.sum(grad_zed * bn_hat, axis=0)),...  30.2 us
    ppermute x7, starting transfers between devices, bench_launch(): jax.lax.ppermute(after[-1] if after else values, named_axis, vals)  27.5 us
  transfers between devices with their start and end apart: 26, of which 12 were waited for; matrix products, arithmetic and copies ran while one was open for 9% of the time, Pallas kernels for 0%

profile of v1, /device:TPU:0, one launch (start us, length us, event | category | flops | bytes accessed | tf_op | source)
XLA Modules:
  0.0 454.7 jit_solution(520971405363538209)
XLA Ops:
  8.4 5.1 %collective-permute-start.8 = (f32[31,64]{1,0:T(8,128)}, f32[31,64]{1,0:T(8,128)S(1)}, u32[]{:S(2)}, u32[]{:S(2)}) collective-permute-start(f32[31,64]{1,0:T(8,128)} %param.14), channel_id=1, source_target_pairs={{1,0},{2,1},{3,2},{4,3},{5,4},{6,5},{7,6},{8,7},{9,8},{10,9},{11,1... | collective-permute-start | bytes 23816 | tf_op jit(solution)/shard_map/ppermute | solution.py:26
  14.2 1.3 collective-permute-start.16
  15.5 1.3 collective-permute-start.18
  16.9 1.1 convert_reduce_fusion
  18.0 1.2 collective-permute-start.1
  19.2 1.2 fusion.129
  20.3 3.7 collective-permute-done.1
  24.0 4.4 collective-permute-start.9
  28.5 1.7 collective-permute-done.2
  30.2 4.5 collective-permute-start.10
  34.7 1.5 collective-permute-done.3
  36.2 1.3 fusion.301
  38.2 0.9 dynamic-update-slice.2
  39.0 0.8 dynamic-update-slice
  39.9 0.8 dynamic-update-slice.1
  40.7 34.3 %all-reduce = f32[1024]{0:T(1024)S(1)} all-reduce(f32[1024]{0:T(1024)S(1)} %dynamic-update-slice), channel_id=1, replica_groups=mesh['mix'=2,'seq'=16] {'seq'}, use_global_device_ids=true, to_apply=%add | all-reduce | flops 1024 | bytes 8192
  75.6 0.9 collective-permute-done.11
  76.5 4.5 collective-permute-start.12
  81.1 0.7 compare_convert_fusion.29
  82.5 4.5 collective-permute-start.13
  87.0 0.7 compare_convert_fusion.14
  87.7 0.7 collective-permute-done.13
  88.4 4.4 collective-permute-start.14
  93.0 0.7 constant_dynamic-update-slice_fusion.7
  95.3 3.1 fusion.293
  98.6 1.3 collective-permute-start.15
  99.9 1.3 collective-permute-start.17
  103.7 4.8 %fusion.296 = (f32[1024]{0:T(1024)S(1)}, f32[1024]{0:T(1024)S(1)}, f32[128,1024]{1,0:T(8,128)S(1)}) fusion(f32[128]{0:T(128)S(1)} %get-tuple-element.110, bf16[15,1024]{1,0:T(8,128)(2,1)S(1)} %collective-permute-done.17, bf16[128,1024]{1,0:T(8,128)(2,1)S(1)} %multiply_convert_fusion.3, f32[1024]{0:T(1024)S(1)} %mul.1492, f32[128]{0:T(128)S(1)} %get-tuple-element.111, ...), kind=kLoop, calls=%fused_computation.560 | loop fusion | flops 28178432 | bytes 998400 | tf_op jit(solution)/shard_map/reduce_sum | solution.py:97
  108.5 63.9 %all-reduce.5 = (f32[1024]{0:T(1024)S(1)}, f32[1024]{0:T(1024)S(1)}, f32[1024]{0:T(1024)S(1)}, f32[1024]{0:T(1024)S(1)}) all-reduce(f32[1024]{0:T(1024)S(1)} %dynamic-update-slice.2, f32[1024]{0:T(1024)S(1)} %dynamic-update-slice.1, f32[1024]{0:T(1024)S(1)} %get-tuple-element.45, ...), channel_id=1, replica_groups=mesh['mix'=2,'seq'=16] {'seq'}, use_global_device_ids=true, to_apply=%add.2 | all-reduce | flops 4096 | bytes 32768
  172.4 2.5 fusion.295
  175.0 30.2 %all-reduce.4 = (f32[1024]{0:T(1024)S(1)}, f32[1024]{0:T(1024)S(1)}) all-reduce(f32[1024]{0:T(1024)S(1)} %get-tuple-element.43, f32[1024]{0:T(1024)S(1)} %get-tuple-element.42), channel_id=1, replica_groups=mesh['mix'=2,'seq'=16] {'seq'}, use_global_device_ids=true, to_apply=%region_9.10 | all-reduce | flops 2048 | bytes 16384 | tf_op jit(solution)/shard_map/psum | solution.py:127
  205.2 0.9 fusion.250
  206.7 0.7 fusion.247
  207.5 0.7 fusion.180
  209.1 1.0 copy.17
  210.2 2.7 convolution_multiply_fusion.1
  213.0 1.3 collective-permute-start.19
  214.3 3.0 collective-permute-start.20
  217.4 0.9 collective-permute-done.20
  218.2 4.3 multiply_convert_fusion.1
  222.8 4.6 %convolution_multiply_fusion = f32[1024,2048]{1,0:T(8,128)} fusion(bf16[128,1024]{1,0:T(8,128)(2,1)S(1)} %multiply_convert_fusion, bf16[128,1024]{1,0:T(8,128)(2,1)S(1)} %get-tuple-element.84, bf16[128,1024]{1,0:T(8,128)(2,1)S(1)} %copy-done, f32[1024]{0:T(1024)S(1)} %all-reduce, f32[128]{0:T(128)S(1)} %add_rsqrt_fusion.1, f32[128]{0:T(128)S(1)} %broadcast_multiply_fusion.6), kind=kOutput, calls=%fused_computation.1 | convolution fusion | flops 540672000 | bytes 9180160 | tf_op jit(solution)/shard_map/fa,fb->ab/dot_general | solution.py:162
  228.6 3.1 fusion.1
  231.8 1.7 fusion.128
  233.5 31.1 %all-reduce.3 = f32[1024]{0:T(1024)S(1)} all-reduce(f32[1024]{0:T(1024)S(1)} %broadcast_multiply_fusion.1), channel_id=5, replica_groups=mesh['mix'=2,'seq'=16] {'seq'}, use_global_device_ids=true, to_apply=%region_47.48.clone | all-reduce | flops 1024 | bytes 8192
  265.2 1.0 fusion.127
  266.2 1.4 copy.18
  267.6 72.4 %reduce-scatter.8.cloned.1.call-done = f32[64,1024]{1,0:T(8,128)} async-done(((f32[1024,1024]{1,0:T(8,128)}), f32[64,1024]{1,0:T(8,128)}) %reduce-scatter.8.cloned.1.call-update) | async-done | bytes 262160 | tf_op jit(solution)/shard_map/reduce_scatter | solution.py:113
  340.0 108.1 %reduce-scatter.6.cloned.1.call-done = f32[64,2048]{1,0:T(8,128)} async-done(((f32[1024,2048]{1,0:T(8,128)}), f32[64,2048]{1,0:T(8,128)}) %reduce-scatter.6.cloned.1.call-update) | async-done | bytes 524304 | tf_op jit(solution)/shard_map/reduce_scatter | solution.py:166
  (116 shorter events, 10.9 us)
Async XLA Ops:
  7.2 88.1 %all-gather.3.cloned.1.call-start = ((), (), s32[]{:S(2)}) async-start(), calls=%async_computation.3 | async-start | bytes 4456448 | tf_op jit(solution)/shard_map/all_gather | solution.py:82
  7.9 164.5 %all-gather.5.cloned.1.call-start = ((), (), s32[]{:S(2)}) async-start(), calls=%async_computation.4 | async-start | bytes 2228224 | tf_op jit(solution)/shard_map/all_gather | solution.py:109
  7.9 10.0 %collective-permute-start = (f32[31,64]{1,0:T(8,128)}, f32[31,64]{1,0:T(8,128)S(1)}, u32[]{:S(2)}, u32[]{:S(2)}) collective-permute-start(f32[31,64]{1,0:T(8,128)} %param.14), channel_id=1, source_target_pairs={{0,1},{1,2},{2,3},{3,4},{4,5},{5,6},{6,7},{7,8},{8,9},{9,10},{10,1... | collective-permute-start | bytes 23816 | tf_op jit(solution)/shard_map/ppermute | solution.py:23
  8.4 15.6 %collective-permute-start.8 = (f32[31,64]{1,0:T(8,128)}, f32[31,64]{1,0:T(8,128)S(1)}, u32[]{:S(2)}, u32[]{:S(2)}) collective-permute-start(f32[31,64]{1,0:T(8,128)} %param.14), channel_id=1, source_target_pairs={{1,0},{2,1},{3,2},{4,3},{5,4},{6,5},{7,6},{8,7},{9,8},{10,9},{11,1... | collective-permute-start | bytes 23816 | tf_op jit(solution)/shard_map/ppermute | solution.py:26
  14.2 61.3 %collective-permute-start.16 = (s32[15]{0:T(128)S(1)}, s32[15]{0:T(128)S(1)}, u32[]{:S(2)}, u32[]{:S(2)}) collective-permute-start(s32[15]{0:T(128)S(1)} %get-tuple-element.128), channel_id=1, source_target_pairs={{0,1},{1,2},{2,3},{3,4},{4,5},{5,6},{6,7},{7,8},{8,9},{9,10},{10,1... | collective-permute-start | bytes 188 | tf_op jit(solution)/shard_map/ppermute | solution.py:44
  15.5 60.0 %collective-permute-start.18 = (s32[15]{0:T(128)S(1)}, s32[15]{0:T(128)S(1)}, u32[]{:S(2)}, u32[]{:S(2)}) collective-permute-start(s32[15]{0:T(128)S(1)} %get-tuple-element.129), channel_id=1, source_target_pairs={{1,0},{2,1},{3,2},{4,3},{5,4},{6,5},{7,6},{8,7},{9,8},{10,9},{11,1... | collective-permute-start | bytes 188 | tf_op jit(solution)/shard_map/ppermute | solution.py:46
  16.9 249.3 %reduce-scatter.10.cloned.1.call-start = ((), (), s32[]{:S(2)}) async-start(), calls=%async_computation.7 | async-start | bytes 557056
  18.0 6.0 %collective-permute-start.1 = (f32[31,64]{1,0:T(8,128)S(1)}, f32[31,64]{1,0:T(8,128)S(1)}, u32[]{:S(2)}, u32[]{:S(2)}) collective-permute-start(f32[31,64]{1,0:T(8,128)S(1)} %collective-permute-done), channel_id=1, source_target_pairs={{0,1},{1,2},{2,3},{3,4},{4,5},{5,6},{6,7},{7,8},{8,9},{9,10},{10,1... | collective-permute-start | bytes 23816 | tf_op jit(solution)/shard_map/ppermute | solution.py:23
  24.0 6.1 %collective-permute-start.2 = (f32[31,64]{1,0:T(8,128)S(1)}, f32[31,64]{1,0:T(8,128)S(1)}, u32[]{:S(2)}, u32[]{:S(2)}) collective-permute-start(f32[31,64]{1,0:T(8,128)S(1)} %collective-permute-done.1), channel_id=1, source_target_pairs={{0,1},{1,2},{2,3},{3,4},{4,5},{5,6},{6,7},{7,8},{8,9},{9,10},{10,1... | collective-permute-start | bytes 23816 | tf_op jit(solution)/shard_map/ppermute | solution.py:23
  24.0 6.2 %collective-permute-start.9 = (f32[31,64]{1,0:T(8,128)S(1)}, f32[31,64]{1,0:T(8,128)S(1)}, u32[]{:S(2)}, u32[]{:S(2)}) collective-permute-start(f32[31,64]{1,0:T(8,128)S(1)} %collective-permute-done.8), channel_id=1, source_target_pairs={{1,0},{2,1},{3,2},{4,3},{5,4},{6,5},{7,6},{8,7},{9,8},{10,9},{11,1... | collective-permute-start | bytes 23816 | tf_op jit(solution)/shard_map/ppermute | solution.py:26
  30.2 6.0 %collective-permute-start.3 = (f32[31,64]{1,0:T(8,128)S(1)}, f32[31,64]{1,0:T(8,128)S(1)}, u32[]{:S(2)}, u32[]{:S(2)}) collective-permute-start(f32[31,64]{1,0:T(8,128)S(1)} %collective-permute-done.2), channel_id=1, source_target_pairs={{0,1},{1,2},{2,3},{3,4},{4,5},{5,6},{6,7},{7,8},{8,9},{9,10},{10,1... | collective-permute-start | bytes 23816 | tf_op jit(solution)/shard_map/ppermute | solution.py:23
  30.2 44.8 %collective-permute-start.10 = (f32[31,64]{1,0:T(8,128)S(1)}, f32[31,64]{1,0:T(8,128)S(1)}, u32[]{:S(2)}, u32[]{:S(2)}) collective-permute-start(f32[31,64]{1,0:T(8,128)S(1)} %collective-permute-done.9), channel_id=1, source_target_pairs={{1,0},{2,1},{3,2},{4,3},{5,4},{6,5},{7,6},{8,7},{9,8},{10,9},{11,1... | collective-permute-start | bytes 23816 | tf_op jit(solution)/shard_map/ppermute | solution.py:26
  36.2 38.9 %collective-permute-start.4 = (f32[31,64]{1,0:T(8,128)S(1)}, f32[31,64]{1,0:T(8,128)S(1)}, u32[]{:S(2)}, u32[]{:S(2)}) collective-permute-start(f32[31,64]{1,0:T(8,128)S(1)} %collective-permute-done.3), channel_id=1, source_target_pairs={{0,1},{1,2},{2,3},{3,4},{4,5},{5,6},{6,7},{7,8},{8,9},{9,10},{10,1... | collective-permute-start | bytes 23816 | tf_op jit(solution)/shard_map/ppermute | solution.py:23
  75.0 1.5 collective-permute-start.11
  75.1 6.0 %collective-permute-start.5 = (f32[31,64]{1,0:T(8,128)S(1)}, f32[31,64]{1,0:T(8,128)S(1)}, u32[]{:S(2)}, u32[]{:S(2)}) collective-permute-start(f32[31,64]{1,0:T(8,128)S(1)} %collective-permute-done.4), channel_id=1, source_target_pairs={{0,1},{1,2},{2,3},{3,4},{4,5},{5,6},{6,7},{7,8},{8,9},{9,10},{10,1... | collective-permute-start | bytes 23816 | tf_op jit(solution)/shard_map/ppermute | solution.py:23
  76.5 5.9 %collective-permute-start.12 = (f32[31,64]{1,0:T(8,128)S(1)}, f32[31,64]{1,0:T(8,128)S(1)}, u32[]{:S(2)}, u32[]{:S(2)}) collective-permute-start(f32[31,64]{1,0:T(8,128)S(1)} %collective-permute-done.11), channel_id=1, source_target_pairs={{1,0},{2,1},{3,2},{4,3},{5,4},{6,5},{7,6},{8,7},{9,8},{10,9},{11,1... | collective-permute-start | bytes 23816 | tf_op jit(solution)/shard_map/ppermute | solution.py:26
  81.1 5.9 %collective-permute-start.6 = (f32[31,64]{1,0:T(8,128)S(1)}, f32[31,64]{1,0:T(8,128)S(1)}, u32[]{:S(2)}, u32[]{:S(2)}) collective-permute-start(f32[31,64]{1,0:T(8,128)S(1)} %collective-permute-done.5), channel_id=1, source_target_pairs={{0,1},{1,2},{2,3},{3,4},{4,5},{5,6},{6,7},{7,8},{8,9},{9,10},{10,1... | collective-permute-start | bytes 23816 | tf_op jit(solution)/shard_map/ppermute | solution.py:23
  82.5 6.0 %collective-permute-start.13 = (f32[31,64]{1,0:T(8,128)S(1)}, f32[31,64]{1,0:T(8,128)S(1)}, u32[]{:S(2)}, u32[]{:S(2)}) collective-permute-start(f32[31,64]{1,0:T(8,128)S(1)} %collective-permute-done.12), channel_id=1, source_target_pairs={{1,0},{2,1},{3,2},{4,3},{5,4},{6,5},{7,6},{8,7},{9,8},{10,9},{11,1... | collective-permute-start | bytes 23816 | tf_op jit(solution)/shard_map/ppermute | solution.py:26
  87.0 6.0 %collective-permute-start.7 = (f32[31,64]{1,0:T(8,128)S(1)}, f32[31,64]{1,0:T(8,128)S(1)}, u32[]{:S(2)}, u32[]{:S(2)}) collective-permute-start(f32[31,64]{1,0:T(8,128)S(1)} %collective-permute-done.6), channel_id=1, source_target_pairs={{0,1},{1,2},{2,3},{3,4},{4,5},{5,6},{6,7},{7,8},{8,9},{9,10},{10,1... | collective-permute-start | bytes 23816 | tf_op jit(solution)/shard_map/ppermute | solution.py:23
  88.4 5.9 %collective-permute-start.14 = (f32[31,64]{1,0:T(8,128)S(1)}, f32[31,64]{1,0:T(8,128)S(1)}, u32[]{:S(2)}, u32[]{:S(2)}) collective-permute-start(f32[31,64]{1,0:T(8,128)S(1)} %collective-permute-done.13), channel_id=1, source_target_pairs={{1,0},{2,1},{3,2},{4,3},{5,4},{6,5},{7,6},{8,7},{9,8},{10,9},{11,1... | collective-permute-start | bytes 23816 | tf_op jit(solution)/shard_map/ppermute | solution.py:26
  95.3 77.1 %copy-start.2 = (bf16[128,1024]{1,0:T(8,128)(2,1)S(1)}, bf16[128,1024]{1,0:T(8,128)(2,1)}, u32[]{:S(2)}) copy-start(bf16[128,1024]{1,0:T(8,128)(2,1)} %param.11) | copy-start | bytes 786436
  98.6 5.1 %collective-permute-start.15 = (bf16[15,1024]{1,0:T(8,128)(2,1)S(1)}, bf16[15,1024]{1,0:T(8,128)(2,1)S(1)}, u32[]{:S(2)}, u32[]{:S(2)}) collective-permute-start(bf16[15,1024]{1,0:T(8,128)(2,1)S(1)} %get-tuple-element.89), channel_id=1, source_target_pairs={{0,1},{1,2},{2,3},{3,4},{4,5},{5,6},{6,7},{7,8},{8,9},{9,10},{10,1... | collective-permute-start | bytes 92168 | tf_op jit(solution)/shard_map/ppermute | solution.py:44
  99.9 3.8 collective-permute-start.17
  210.1 129.9 %reduce-scatter.8.cloned.1.call-start = ((), (), s32[]{:S(2)}) async-start(), calls=%async_computation.6 | async-start | bytes 4456448 | tf_op jit(solution)/shard_map/reduce_scatter | solution.py:113
  212.9 9.8 %copy-start = (bf16[128,1024]{1,0:T(8,128)(2,1)S(1)}, bf16[128,1024]{1,0:T(8,128)(2,1)}, u32[]{:S(2)}) copy-start(bf16[128,1024]{1,0:T(8,128)(2,1)} %param.9) | copy-start | bytes 786436
  212.9 235.2 %reduce-scatter.6.cloned.1.call-start = ((), (), s32[]{:S(2)}) async-start(), calls=%async_computation.5 | async-start | bytes 8912896 | tf_op jit(solution)/shard_map/reduce_scatter | solution.py:166
  213.0 4.3 collective-permute-start.19
  214.3 3.9 collective-permute-start.20
  228.0 3.7 copy-start.1
Sparse Core Ops, SparseCore 0:
  10.2 53.9 all-gather.2
  66.4 40.2 all-gather.4
  210.2 53.1 reduce-scatter.9
  268.2 71.7 reduce-scatter.7
  344.5 103.5 reduce-scatter.5
